TPU v7x, 512 devices: a whole 4x4x16 slice. The times are simulated.
512 devices in a mesh: ctx: 64 (over x, y, z_hi, core), head: 8 (over z_lo).
Axes of the slice: x: 4, y: 4, z: 16 (z_hi: 2, z_lo: 8; z = z_hi * 8 + z_lo), core: 2. Of those that a mesh axis runs over, the one named last changes fastest.
Arguments:
- query_head_rows: bfloat16 [16384, 4096], P('ctx', 'head'), may hold values from -4 to 4
- key_head_rows: bfloat16 [16384, 1024], P('ctx', 'head'), may hold values from -4 to 4
- value_head_rows: bfloat16 [16384, 1024], P('ctx', 'head'), may hold values from -4 to 4
- forward_output: bfloat16 [16384, 4096], P('ctx', 'head'), may hold values from -4 to 4, as said below
- cotangent: bfloat16 [16384, 4096], P('ctx', 'head'), may hold values from -6 to 6
- logsumexp: float32 [32, 16384], P('head', 'ctx'), as said below
- document_lengths: int32 [64], replicated, may hold values from 1 to 768, as said below
- linear_row_index: int32 [16384], replicated, may hold values from 0 to 16383, as said below
Outputs:
- query_gradient: bfloat16 [16384, 4096], P(('ctx', 'head'))
- linear_key_gradient: bfloat16 [16384, 1024], P(('ctx', 'head'))
- linear_value_gradient: bfloat16 [16384, 1024], P(('ctx', 'head'))
Inputs may be any that keep to these rules, and one draw needn't show every extreme that they name: `logsumexp`: for each head and position, the log of the sum of exp(scores) over the keys that the position sees, from the forward pass on these query_head_rows and key_head_rows. `forward_output`: for each head, the forward pass's softmax weights times value_head_rows, rounded to bfloat16. `document_lengths`: the lengths sum to 16384; the longest document has exactly 768 tokens. `linear_row_index`: A permutation of the 16384 positions. Counting positions in blocks of 256, from one block of the packed sequence at most 8 rows go to one block of linear positions, some pair of blocks reaches 8, and every linear block receives 256 rows.
All inputs are finite; a program needn't handle non-finite values.
Results may differ from a plain program's by a relative error of at most 0.0049.
Values may be sent and summed in bfloat16 or wider, within the bound.
No kernel may reach another device: no remote copies, remote signals or barrier semaphores. Data moves between devices by JAX's collectives and lax.ppermute only.
A program may use at most 64 MiB of HBM per device.

v0:
```python
import jax
import jax.numpy as jnp
from jax import lax
from jax.sharding import PartitionSpec as P

HEAD_SIZE = 128
DOC_BLOCKS = 3


def from_behind(shard, axis, by):
    count = lax.axis_size(axis)
    pairs = [(i, i + by) for i in range(count) if 0 <= i + by < count]
    return lax.ppermute(shard, axis, pairs)


def shifted(block, axis, distance):
    devices = range(lax.axis_size(axis))
    route = [((i - distance) % len(devices), i) for i in devices]
    return lax.ppermute(block, axis, route)


def block_grads(
    query_vectors,
    output_gradient,
    log_normalizer,
    row_correction,
    begins,
    query_pos,
    key_part,
    value_part,
    key_start,
):
    length = query_vectors.shape[0]
    kv_heads = query_vectors.shape[1]
    scaling = HEAD_SIZE ** (-0.5)
    key_heads = key_part.reshape(length, kv_heads, HEAD_SIZE)
    value_heads = value_part.reshape(length, kv_heads, HEAD_SIZE)
    scores = (
        jnp.einsum("qngd,knd->qngk", query_vectors, key_heads, preferred_element_type=jnp.float32)
        * scaling
    )
    key_pos = key_start + lax.iota(jnp.int32, length)
    visible = (key_pos[None, :] <= query_pos[:, None]) & (key_pos[None, :] >= begins[:, None])
    weights = jnp.exp(
        jnp.where(visible[:, None, None, :], scores - log_normalizer[..., None], -jnp.inf)
    )
    weights_low = weights.astype(jnp.bfloat16)
    grad_weights = jnp.einsum(
        "qngd,knd->qngk", output_gradient, value_heads, preferred_element_type=jnp.float32
    )
    grad_scores = (weights * (grad_weights - row_correction[..., None]) * scaling).astype(
        jnp.bfloat16
    )
    query_term = jnp.einsum(
        "qngk,knd->qngd", grad_scores, key_heads, preferred_element_type=jnp.float32
    )
    key_term = jnp.einsum(
        "qngk,qngd->knd", grad_scores, query_vectors, preferred_element_type=jnp.float32
    )
    value_term = jnp.einsum(
        "qngk,qngd->knd", weights_low, output_gradient, preferred_element_type=jnp.float32
    )
    return (query_term, key_term.reshape(length, -1), value_term.reshape(length, -1))


def per_device(
    query_head_rows,
    key_head_rows,
    value_head_rows,
    forward_output,
    cotangent,
    logsumexp,
    document_lengths,
    linear_row_index,
):
    length = query_head_rows.shape[0]
    kv_heads = key_head_rows.shape[1] // HEAD_SIZE
    query_groups = logsumexp.shape[0] // kv_heads
    block_index = lax.axis_index("ctx")
    blocks = lax.axis_size("ctx")
    query_pos = block_index * length + lax.iota(jnp.int32, length)
    finish = jnp.cumsum(document_lengths)
    firsts = finish - document_lengths
    begins = jnp.max(jnp.where(firsts[None, :] <= query_pos[:, None], firsts[None, :], 0), axis=1)
    query_vectors = query_head_rows.reshape(length, kv_heads, query_groups, HEAD_SIZE)
    output_gradient = cotangent.reshape(length, kv_heads, query_groups, HEAD_SIZE)
    log_normalizer = logsumexp.T.reshape(length, kv_heads, query_groups)
    row_correction = jnp.sum(
        output_gradient.astype(jnp.float32)
        * forward_output.reshape(length, kv_heads, query_groups, HEAD_SIZE).astype(jnp.float32),
        axis=3,
    )

    def block_terms(key_part, value_part, distance):
        key_start = (block_index - distance) * length
        return block_grads(
            query_vectors,
            output_gradient,
            log_normalizer,
            row_correction,
            begins,
            query_pos,
            key_part,
            value_part,
            key_start,
        )

    query_acc, key_running_sum, value_running_sum = block_terms(key_head_rows, value_head_rows, 0)
    moving_keys, moving_values = (key_head_rows, value_head_rows)
    for distance in range(1, DOC_BLOCKS + 1):
        moving_keys, moving_values = from_behind((moving_keys, moving_values), "ctx", 1)
        key_running_sum, value_running_sum = shifted((key_running_sum, value_running_sum), "ctx", 1)
        query_term, key_term, value_term = block_terms(moving_keys, moving_values, distance)
        query_acc = query_acc + query_term
        key_running_sum = key_running_sum + key_term
        value_running_sum = value_running_sum + value_term
    key_running_sum, value_running_sum = (
        shifted(key_running_sum.astype(jnp.bfloat16), "ctx", -DOC_BLOCKS).astype(
            key_running_sum.dtype
        ),
        shifted(value_running_sum.astype(jnp.bfloat16), "ctx", -DOC_BLOCKS).astype(
            value_running_sum.dtype
        ),
    )
    query_grad = query_acc.reshape(length, -1).astype(jnp.bfloat16)
    key_row_gradient = key_running_sum.astype(jnp.bfloat16)
    value_row_gradient = value_running_sum.astype(jnp.bfloat16)
    capacity = 2 * length // blocks
    own_targets = lax.dynamic_slice_in_dim(linear_row_index, block_index * length, length)
    target = own_targets // length
    owner_marks = (target[:, None] == lax.iota(jnp.int32, blocks)[None, :]).astype(jnp.int32)
    slot_rank = jnp.sum(owner_marks * (jnp.cumsum(owner_marks, axis=0) - 1), axis=1)
    send_slots = target * capacity + slot_rank

    def pack_slots(grad_rows):
        return (
            jnp.zeros((blocks * capacity, grad_rows.shape[1]), grad_rows.dtype)
            .at[send_slots]
            .set(grad_rows)
        )

    arrived = (
        lax.all_to_all(pack_slots(query_grad), "ctx", split_axis=0, concat_axis=0, tiled=True),
        lax.all_to_all(
            pack_slots(key_row_gradient), "ctx", split_axis=0, concat_axis=0, tiled=True
        ),
        lax.all_to_all(
            pack_slots(value_row_gradient), "ctx", split_axis=0, concat_axis=0, tiled=True
        ),
    )
    all_owners = linear_row_index.reshape(blocks, length)
    landing = all_owners // length == block_index
    landed_rank = jnp.cumsum(landing.astype(jnp.int32), axis=1) - 1
    source_slot = lax.iota(jnp.int32, blocks)[:, None] * capacity + landed_rank
    where_to = jnp.where(landing, all_owners % length, length)
    inverse = (
        jnp.zeros((length,), jnp.int32)
        .at[where_to.reshape(-1)]
        .set(source_slot.reshape(-1), mode="drop")
    )
    linear_query = arrived[0][inverse]
    linear_key = arrived[1][inverse]
    linear_value = arrived[2][inverse]
    result = (
        lax.all_to_all(linear_query, "head", split_axis=0, concat_axis=1, tiled=True),
        lax.all_to_all(linear_key, "head", split_axis=0, concat_axis=1, tiled=True),
        lax.all_to_all(linear_value, "head", split_axis=0, concat_axis=1, tiled=True),
    )
    return (result[0], result[1], result[2])


def solution(mesh):
    placed = (
        P("ctx", "head"),
        P("ctx", "head"),
        P("ctx", "head"),
        P("ctx", "head"),
        P("ctx", "head"),
        P("head", "ctx"),
        P(),
        P(),
    )
    return jax.shard_map(
        per_device,
        mesh=mesh,
        in_specs=placed,
        out_specs=(P(("ctx", "head"), None), P(("ctx", "head"), None), P(("ctx", "head"), None)),
        check_vma=False,
    )
```

profile of v0, /device:TPU:32, one launch (start us, length us, event | category | flops | bytes accessed | tf_op | source)
XLA Modules:
  0.0 360.1 jit_solution(3413833666730126142)
XLA Ops:
  0.6 1.9 collective-permute-start.1
  2.5 15.1 %collective-permute-start = (bf16[256,128]{1,0:T(8,128)(2,1)}, bf16[256,128]{1,0:T(8,128)(2,1)S(1)}, u32[]{:S(2)}, u32[]{:S(2)}) collective-permute-start(bf16[256,128]{1,0:T(8,128)(2,1)} %param.9), channel_id=1, source_target_pairs={{0,8},{8,16},{16,24},{24,32},{32,40},{40,48},{48,56},{56,64},{64,7... | collective-permute-start | bytes 196616 | tf_op jit(solution)/shard_map/ppermute | solution.py:13
  17.7 0.6 copy-done.14
  18.6 1.1 convert_multiply_fusion
  20.8 0.5 copy-done.6
  21.7 0.6 copy-done.1
  22.9 2.1 collective-permute-start.6
  25.2 1.9 collective-permute-start.10
  27.4 1.1 fusion.89
  28.5 0.6 reduce-window.24
  29.7 0.6 reduce-window.32
  30.7 60.3 %scatter_custom_fusion.1 = s32[256]{0:T(256)S(1)} fusion(s32[16384]{0:T(1024)S(1)} %compare_select_fusion, s32[16384]{0:T(1024)S(1)} %add.156, s32[]{:T(128)} %constant.73.clone.1), kind=kCustom, calls=%fused_computation.185 | custom fusion | bytes 1028 | tf_op jit(solution)/shard_map/scatter | solution.py:159
  91.0 1.9 collective-permute-start.3
  93.0 13.9 %collective-permute-start.2 = (bf16[256,128]{1,0:T(8,128)(2,1)S(1)}, bf16[256,128]{1,0:T(8,128)(2,1)S(1)}, u32[]{:S(2)}, u32[]{:S(2)}) collective-permute-start(bf16[256,128]{1,0:T(8,128)(2,1)S(1)} %collective-permute-done), channel_id=1, source_target_pairs={{0,8},{8,16},{16,24},{24,32},{32,40},{40,48},{48,56},{56,64},{64,7... | collective-permute-start | bytes 196616 | tf_op jit(solution)/shard_map/ppermute | solution.py:13
  107.8 2.3 collective-permute-start.4
  110.1 0.4 fusion.31
  111.4 16.5 %collective-permute-start.7 = (f32[256,128]{1,0:T(8,128)S(1)}, f32[256,128]{1,0:T(8,128)S(1)}, u32[]{:S(2)}, u32[]{:S(2)}) collective-permute-start(f32[256,128]{1,0:T(8,128)S(1)} %fusion.45), channel_id=1, source_target_pairs={{504,0},{0,8},{8,16},{16,24},{24,32},{32,40},{40,48},{48,56},{56,6... | collective-permute-start | bytes 393224 | tf_op jit(solution)/shard_map/ppermute | solution.py:19
  127.9 1.9 collective-permute-start.5
  131.0 4.1 %collective-permute-done.7 = f32[256,128]{1,0:T(8,128)S(1)} collective-permute-done((f32[256,128]{1,0:T(8,128)S(1)}, f32[256,128]{1,0:T(8,128)S(1)}, u32[]{:S(2)}, u32[]{:S(2)}) %collective-permute-start.7) | collective-permute-done | bytes 131104 | tf_op jit(solution)/shard_map/ppermute | solution.py:19
  135.1 1.9 collective-permute-start.8
  137.4 18.8 %collective-permute-done.8 = f32[256,128]{1,0:T(8,128)S(1)} collective-permute-done((f32[256,128]{1,0:T(8,128)S(1)}, f32[256,128]{1,0:T(8,128)S(1)}, u32[]{:S(2)}, u32[]{:S(2)}) %collective-permute-start.8) | collective-permute-done | bytes 131104 | tf_op jit(solution)/shard_map/ppermute | solution.py:19
  156.2 1.9 collective-permute-start.9
  158.4 12.3 %collective-permute-start.11 = (f32[256,128]{1,0:T(8,128)S(1)}, f32[256,128]{1,0:T(8,128)S(1)}, u32[]{:S(2)}, u32[]{:S(2)}) collective-permute-start(f32[256,128]{1,0:T(8,128)S(1)} %fusion.46), channel_id=1, source_target_pairs={{504,0},{0,8},{8,16},{16,24},{24,32},{32,40},{40,48},{48,56},{56,6... | collective-permute-start | bytes 393224 | tf_op jit(solution)/shard_map/ppermute | solution.py:19
  170.8 2.1 scatter_custom_fusion.2
  172.8 21.6 %all-to-all-start.2 = ((bf16[64,8,128]{2,1,0:T(8,128)(2,1)}), bf16[64,8,128]{2,1,0:T(8,128)(2,1)S(1)}, u32[]{:S(2)}, u32[]{:S(2)}) async-start(bf16[64,8,128]{2,1,0:T(8,128)(2,1)} %bitcast.50), calls=%async_computation.2 | async-start | bytes 262144 | tf_op jit(solution)/shard_map/all_to_all | solution.py:144
  194.8 2.0 collective-permute-start.12
  197.0 21.8 %collective-permute-done.12 = f32[256,128]{1,0:T(8,128)S(1)} collective-permute-done((f32[256,128]{1,0:T(8,128)S(1)}, f32[256,128]{1,0:T(8,128)S(1)}, u32[]{:S(2)}, u32[]{:S(2)}) %collective-permute-start.12) | collective-permute-done | bytes 131104 | tf_op jit(solution)/shard_map/ppermute | solution.py:19
  218.9 1.9 collective-permute-start.13
  220.8 12.4 %collective-permute-done.13 = bf16[256,128]{1,0:T(8,128)(2,1)S(1)} collective-permute-done((bf16[256,128]{1,0:T(8,128)(2,1)S(1)}, bf16[256,128]{1,0:T(8,128)(2,1)S(1)}, u32[]{:S(2)}, u32[]{:S(2)}) %collective-permute-start.13) | collective-permute-done | bytes 65568 | tf_op jit(solution)/shard_map/ppermute | solution.py:19
  233.2 1.8 scatter_custom_fusion.3
  235.0 15.5 %all-to-all-start.4 = ((bf16[64,8,128]{2,1,0:T(8,128)(2,1)}), bf16[64,8,128]{2,1,0:T(8,128)(2,1)S(1)}, u32[]{:S(2)}, u32[]{:S(2)}) async-start(bf16[64,8,128]{2,1,0:T(8,128)(2,1)} %bitcast.62), calls=%async_computation.4 | async-start | bytes 262144 | tf_op jit(solution)/shard_map/all_to_all | solution.py:147
  250.8 0.6 copy-done.10
  251.7 1.5 gather_fusion.1
  253.1 16.4 %all-to-all-done.4 = bf16[64,8,128]{2,1,0:T(8,128)(2,1)S(1)} async-done(((bf16[64,8,128]{2,1,0:T(8,128)(2,1)}), bf16[64,8,128]{2,1,0:T(8,128)(2,1)S(1)}, u32[]{:S(2)}, u32[]{:S(2)}) %all-to-all-start.4) | async-done | bytes 131104 | tf_op jit(solution)/shard_map/all_to_all | solution.py:147
  269.5 4.7 %all-to-all-start.3 = ((bf16[8,32,128]{2,1,0:T(8,128)(2,1)}), bf16[8,32,128]{2,1,0:T(8,128)(2,1)S(1)}, u32[]{:S(2)}, u32[]{:S(2)}) async-start(bf16[8,32,128]{2,1,0:T(8,128)(2,1)} %bitcast.52), calls=%async_computation.3 | async-start | bytes 131072 | tf_op jit(solution)/shard_map/all_to_all | solution.py:166
  274.6 2.3 scatter_custom_fusion
  276.9 6.5 %all-to-all-done.3 = bf16[8,32,128]{2,1,0:T(8,128)(2,1)S(1)} async-done(((bf16[8,32,128]{2,1,0:T(8,128)(2,1)}), bf16[8,32,128]{2,1,0:T(8,128)(2,1)S(1)}, u32[]{:S(2)}, u32[]{:S(2)}) %all-to-all-start.3) | async-done | bytes 65568 | tf_op jit(solution)/shard_map/all_to_all | solution.py:166
  283.5 4.6 %all-to-all-start = ((bf16[64,8,512]{2,1,0:T(8,128)(2,1)}), bf16[64,8,512]{2,1,0:T(8,128)(2,1)S(1)}, u32[]{:S(2)}, u32[]{:S(2)}) async-start(bf16[64,8,512]{2,1,0:T(8,128)(2,1)} %bitcast.40), calls=%async_computation | async-start | bytes 1048576 | tf_op jit(solution)/shard_map/all_to_all | solution.py:143
  288.1 1.5 gather_fusion.2
  289.6 36.7 %all-to-all-done = bf16[64,8,512]{2,1,0:T(8,128)(2,1)S(1)} async-done(((bf16[64,8,512]{2,1,0:T(8,128)(2,1)}), bf16[64,8,512]{2,1,0:T(8,128)(2,1)S(1)}, u32[]{:S(2)}, u32[]{:S(2)}) %all-to-all-start) | async-done | bytes 524320 | tf_op jit(solution)/shard_map/all_to_all | solution.py:143
  326.3 3.3 all-to-all-start.5
  329.6 1.9 gather_fusion
  331.4 7.4 %all-to-all-done.5 = bf16[8,32,128]{2,1,0:T(8,128)(2,1)S(1)} async-done(((bf16[8,32,128]{2,1,0:T(8,128)(2,1)}), bf16[8,32,128]{2,1,0:T(8,128)(2,1)S(1)}, u32[]{:S(2)}, u32[]{:S(2)}) %all-to-all-start.5) | async-done | bytes 65568 | tf_op jit(solution)/shard_map/all_to_all | solution.py:167
  338.8 5.0 %all-to-all-start.1 = ((bf16[8,32,512]{2,1,0:T(8,128)(2,1)}), bf16[8,32,512]{2,1,0:T(8,128)(2,1)S(1)}, u32[]{:S(2)}, u32[]{:S(2)}) async-start(bf16[8,32,512]{2,1,0:T(8,128)(2,1)} %bitcast.44), calls=%async_computation.1 | async-start | bytes 524288 | tf_op jit(solution)/shard_map/all_to_all | solution.py:165
  343.8 0.6 copy_bitcast_fusion.1
  344.4 0.6 copy_bitcast_fusion
  345.1 14.3 %all-to-all-done.1 = bf16[8,32,512]{2,1,0:T(8,128)(2,1)S(1)} async-done(((bf16[8,32,512]{2,1,0:T(8,128)(2,1)}), bf16[8,32,512]{2,1,0:T(8,128)(2,1)S(1)}, u32[]{:S(2)}, u32[]{:S(2)}) %all-to-all-start.1) | async-done | bytes 262176 | tf_op jit(solution)/shard_map/all_to_all | solution.py:165
  359.4 0.7 copy.125
  (94 shorter events, 8.8 us)
Async XLA Ops:
  0.6 20.1 %copy-start = (bf16[256,512]{1,0:T(8,128)(2,1)S(1)}, bf16[256,512]{1,0:T(8,128)(2,1)}, u32[]{:S(2)}) copy-start(bf16[256,512]{1,0:T(8,128)(2,1)} %param.8) | copy-start | bytes 786436
  0.6 90.4 %collective-permute-start.1 = (bf16[256,128]{1,0:T(8,128)(2,1)}, bf16[256,128]{1,0:T(8,128)(2,1)S(1)}, u32[]{:S(2)}, u32[]{:S(2)}) collective-permute-start(bf16[256,128]{1,0:T(8,128)(2,1)} %param.10), channel_id=1, source_target_pairs={{0,8},{8,16},{16,24},{24,32},{32,40},{40,48},{48,56},{56,64},{64,7... | collective-permute-start | bytes 196616 | tf_op jit(solution)/shard_map/ppermute | solution.py:13
  2.5 90.5 %collective-permute-start = (bf16[256,128]{1,0:T(8,128)(2,1)}, bf16[256,128]{1,0:T(8,128)(2,1)S(1)}, u32[]{:S(2)}, u32[]{:S(2)}) collective-permute-start(bf16[256,128]{1,0:T(8,128)(2,1)} %param.9), channel_id=1, source_target_pairs={{0,8},{8,16},{16,24},{24,32},{32,40},{40,48},{48,56},{56,64},{64,7... | collective-permute-start | bytes 196616 | tf_op jit(solution)/shard_map/ppermute | solution.py:13
  17.7 0.7 copy-start.14
  20.5 0.8 copy-start.6
  20.5 0.8 copy-start.15
  21.3 1.0 copy-start.1
  21.3 1.0 copy-start.13
  22.9 4.3 %copy-start.5 = (s32[16384]{0:T(1024)S(1)}, s32[16384]{0:T(1024)}, u32[]{:S(2)}) copy-start(s32[16384]{0:T(1024)} %param.15) | copy-start | bytes 196612
  22.9 88.0 %collective-permute-start.6 = (f32[256,128]{1,0:T(8,128)S(1)}, f32[256,128]{1,0:T(8,128)S(1)}, u32[]{:S(2)}, u32[]{:S(2)}) collective-permute-start(f32[256,128]{1,0:T(8,128)S(1)} %convolution_bitcast_fusion.11), channel_id=1, source_target_pairs={{504,0},{0,8},{8,16},{16,24},{24,32},{32,40},{40,48},{48,56},{56,6... | collective-permute-start | bytes 393224 | tf_op jit(solution)/shard_map/ppermute | solution.py:19
  25.2 132.9 %collective-permute-start.10 = (f32[256,128]{1,0:T(8,128)S(1)}, f32[256,128]{1,0:T(8,128)S(1)}, u32[]{:S(2)}, u32[]{:S(2)}) collective-permute-start(f32[256,128]{1,0:T(8,128)S(1)} %convolution_bitcast_fusion.7), channel_id=1, source_target_pairs={{504,0},{0,8},{8,16},{16,24},{24,32},{32,40},{40,48},{48,56},{56,6... | collective-permute-start | bytes 393224 | tf_op jit(solution)/shard_map/ppermute | solution.py:19
  91.0 19.5 %collective-permute-start.3 = (bf16[256,128]{1,0:T(8,128)(2,1)S(1)}, bf16[256,128]{1,0:T(8,128)(2,1)S(1)}, u32[]{:S(2)}, u32[]{:S(2)}) collective-permute-start(bf16[256,128]{1,0:T(8,128)(2,1)S(1)} %collective-permute-done.1), channel_id=1, source_target_pairs={{0,8},{8,16},{16,24},{24,32},{32,40},{40,48},{48,56},{56,64},{64,7... | collective-permute-start | bytes 196616 | tf_op jit(solution)/shard_map/ppermute | solution.py:13
  93.0 14.3 %copy-start.7 = (bf16[256,128]{1,0:T(8,128)(2,1)}, bf16[256,128]{1,0:T(8,128)(2,1)S(1)}, u32[]{:S(2)}) copy-start(bf16[256,128]{1,0:T(8,128)(2,1)S(1)} %collective-permute-done) | copy-start | bytes 196612
  93.0 14.8 %collective-permute-start.2 = (bf16[256,128]{1,0:T(8,128)(2,1)S(1)}, bf16[256,128]{1,0:T(8,128)(2,1)S(1)}, u32[]{:S(2)}, u32[]{:S(2)}) collective-permute-start(bf16[256,128]{1,0:T(8,128)(2,1)S(1)} %collective-permute-done), channel_id=1, source_target_pairs={{0,8},{8,16},{16,24},{24,32},{32,40},{40,48},{48,56},{56,64},{64,7... | collective-permute-start | bytes 196616 | tf_op jit(solution)/shard_map/ppermute | solution.py:13
  107.8 2.7 copy-start.9
  107.8 22.1 %collective-permute-start.4 = (bf16[256,128]{1,0:T(8,128)(2,1)S(1)}, bf16[256,128]{1,0:T(8,128)(2,1)S(1)}, u32[]{:S(2)}, u32[]{:S(2)}) collective-permute-start(bf16[256,128]{1,0:T(8,128)(2,1)S(1)} %collective-permute-done.2), channel_id=1, source_target_pairs={{0,8},{8,16},{16,24},{24,32},{32,40},{40,48},{48,56},{56,64},{64,7... | collective-permute-start | bytes 196616 | tf_op jit(solution)/shard_map/ppermute | solution.py:13
  111.4 23.7 %collective-permute-start.7 = (f32[256,128]{1,0:T(8,128)S(1)}, f32[256,128]{1,0:T(8,128)S(1)}, u32[]{:S(2)}, u32[]{:S(2)}) collective-permute-start(f32[256,128]{1,0:T(8,128)S(1)} %fusion.45), channel_id=1, source_target_pairs={{504,0},{0,8},{8,16},{16,24},{24,32},{32,40},{40,48},{48,56},{56,6... | collective-permute-start | bytes 393224 | tf_op jit(solution)/shard_map/ppermute | solution.py:19
  127.9 2.8 collective-permute-start.5
  129.8 0.6 copy-start.11
  130.4 4.7 %copy-start.2 = (f32[256,1,4,256]{0,3,2,1:T(8,128)}, f32[256,1,4,256]{0,3,2,1:T(8,128)S(1)}, u32[]{:S(2)}) copy-start(f32[256,1,4,256]{0,3,2,1:T(8,128)S(1)} %fusion.35) | copy-start | bytes 3145732
  135.1 21.0 %collective-permute-start.8 = (f32[256,128]{1,0:T(8,128)S(1)}, f32[256,128]{1,0:T(8,128)S(1)}, u32[]{:S(2)}, u32[]{:S(2)}) collective-permute-start(f32[256,128]{1,0:T(8,128)S(1)} %add.159), channel_id=1, source_target_pairs={{504,0},{0,8},{8,16},{16,24},{24,32},{32,40},{40,48},{48,56},{56,6... | collective-permute-start | bytes 393224 | tf_op jit(solution)/shard_map/ppermute | solution.py:19
  156.2 14.5 %collective-permute-start.9 = (bf16[256,128]{1,0:T(8,128)(2,1)S(1)}, bf16[256,128]{1,0:T(8,128)(2,1)}, u32[]{:S(2)}, u32[]{:S(2)}) collective-permute-start(bf16[256,128]{1,0:T(8,128)(2,1)S(1)} %add_convert_fusion.1), channel_id=1, source_target_pairs={{24,0},{32,8},{40,16},{48,24},{56,32},{64,40},{72,48},{80,56},{88,... | collective-permute-start | bytes 196616 | tf_op jit(solution)/shard_map/ppermute | solution.py:19
  158.4 36.3 %collective-permute-start.11 = (f32[256,128]{1,0:T(8,128)S(1)}, f32[256,128]{1,0:T(8,128)S(1)}, u32[]{:S(2)}, u32[]{:S(2)}) collective-permute-start(f32[256,128]{1,0:T(8,128)S(1)} %fusion.46), channel_id=1, source_target_pairs={{504,0},{0,8},{8,16},{16,24},{24,32},{32,40},{40,48},{48,56},{56,6... | collective-permute-start | bytes 393224 | tf_op jit(solution)/shard_map/ppermute | solution.py:19
  172.8 62.1 %all-to-all-start.2 = ((bf16[64,8,128]{2,1,0:T(8,128)(2,1)}), bf16[64,8,128]{2,1,0:T(8,128)(2,1)S(1)}, u32[]{:S(2)}, u32[]{:S(2)}) async-start(bf16[64,8,128]{2,1,0:T(8,128)(2,1)} %bitcast.50), calls=%async_computation.2 | async-start | bytes 262144 | tf_op jit(solution)/shard_map/all_to_all | solution.py:144
  194.4 2.3 copy-start.3
  194.8 24.1 %collective-permute-start.12 = (f32[256,128]{1,0:T(8,128)S(1)}, f32[256,128]{1,0:T(8,128)S(1)}, u32[]{:S(2)}, u32[]{:S(2)}) collective-permute-start(f32[256,128]{1,0:T(8,128)S(1)} %add.162), channel_id=1, source_target_pairs={{504,0},{0,8},{8,16},{16,24},{24,32},{32,40},{40,48},{48,56},{56,6... | collective-permute-start | bytes 393224 | tf_op jit(solution)/shard_map/ppermute | solution.py:19
  197.0 53.5 %copy-start.4 = (f32[256,4,128]{0,2,1:T(8,128)S(1)}, f32[256,4,128]{0,2,1:T(8,128)}, u32[]{:S(2)}) copy-start(f32[256,4,128]{0,2,1:T(8,128)} %fusion.89) | copy-start | bytes 1572868
  218.9 14.3 %collective-permute-start.13 = (bf16[256,128]{1,0:T(8,128)(2,1)S(1)}, bf16[256,128]{1,0:T(8,128)(2,1)S(1)}, u32[]{:S(2)}, u32[]{:S(2)}) collective-permute-start(bf16[256,128]{1,0:T(8,128)(2,1)S(1)} %add_convert_fusion), channel_id=1, source_target_pairs={{24,0},{32,8},{40,16},{48,24},{56,32},{64,40},{72,48},{80,56},{88,... | collective-permute-start | bytes 196616 | tf_op jit(solution)/shard_map/ppermute | solution.py:19
  235.0 15.6 %copy-start.8 = (bf16[256,128]{1,0:T(8,128)(2,1)S(1)}, bf16[256,128]{1,0:T(8,128)(2,1)}, u32[]{:S(2)}) copy-start(bf16[256,128]{1,0:T(8,128)(2,1)} %copy-done.7) | copy-start | bytes 196612
  235.0 34.5 %all-to-all-start.4 = ((bf16[64,8,128]{2,1,0:T(8,128)(2,1)}), bf16[64,8,128]{2,1,0:T(8,128)(2,1)S(1)}, u32[]{:S(2)}, u32[]{:S(2)}) async-start(bf16[64,8,128]{2,1,0:T(8,128)(2,1)} %bitcast.62), calls=%async_computation.4 | async-start | bytes 262144 | tf_op jit(solution)/shard_map/all_to_all | solution.py:147
  250.5 0.8 copy-start.10
  269.5 4.7 %copy-start.12 = (bf16[256,128]{1,0:T(8,128)(2,1)S(1)}, bf16[256,128]{1,0:T(8,128)(2,1)}, u32[]{:S(2)}) copy-start(bf16[256,128]{1,0:T(8,128)(2,1)} %copy-done.11) | copy-start | bytes 196612
  269.5 13.9 %all-to-all-start.3 = ((bf16[8,32,128]{2,1,0:T(8,128)(2,1)}), bf16[8,32,128]{2,1,0:T(8,128)(2,1)S(1)}, u32[]{:S(2)}, u32[]{:S(2)}) async-start(bf16[8,32,128]{2,1,0:T(8,128)(2,1)} %bitcast.52), calls=%async_computation.3 | async-start | bytes 131072 | tf_op jit(solution)/shard_map/all_to_all | solution.py:166
  283.5 42.8 %all-to-all-start = ((bf16[64,8,512]{2,1,0:T(8,128)(2,1)}), bf16[64,8,512]{2,1,0:T(8,128)(2,1)S(1)}, u32[]{:S(2)}, u32[]{:S(2)}) async-start(bf16[64,8,512]{2,1,0:T(8,128)(2,1)} %bitcast.40), calls=%async_computation | async-start | bytes 1048576 | tf_op jit(solution)/shard_map/all_to_all | solution.py:143
  326.3 12.6 %all-to-all-start.5 = ((bf16[8,32,128]{2,1,0:T(8,128)(2,1)}), bf16[8,32,128]{2,1,0:T(8,128)(2,1)S(1)}, u32[]{:S(2)}, u32[]{:S(2)}) async-start(bf16[8,32,128]{2,1,0:T(8,128)(2,1)} %bitcast.64), calls=%async_computation.5 | async-start | bytes 131072 | tf_op jit(solution)/shard_map/all_to_all | solution.py:167
  338.8 20.5 %all-to-all-start.1 = ((bf16[8,32,512]{2,1,0:T(8,128)(2,1)}), bf16[8,32,512]{2,1,0:T(8,128)(2,1)S(1)}, u32[]{:S(2)}, u32[]{:S(2)}) async-start(bf16[8,32,512]{2,1,0:T(8,128)(2,1)} %bitcast.44), calls=%async_computation.1 | async-start | bytes 524288 | tf_op jit(solution)/shard_map/all_to_all | solution.py:165
where the time goes:
time: 361 us; the launch traced here: 360 us
  waiting for transfers between devices  139 us (39%)
  starting transfers between devices  132 us (37%)
  local copies, waits for them, and re-layouts  76.9 us (21%)
  matrix products  6.8 us (2%)
  other arithmetic  4 us (1%)
    scatter x1, local copies, waits for them, and re-layouts, per_device(): inverse = jnp.zeros((length,), jnp.int32).at[where_to.reshape(-1)].set(so...  60.3 us
    ppermute x8, waiting for transfers between devices, shifted(): return lax.ppermute(block, axis, route)  57.1 us
    ppermute x8, starting transfers between devices, shifted(): return lax.ppermute(block, axis, route)  40.5 us
    ppermute x6, starting transfers between devices, from_behind(): return lax.ppermute(shard, axis, pairs)  37 us
    all_to_all x1, waiting for transfers between devices, per_device(): lax.all_to_all(pack_slots(query_grad), 'ctx', split_axis=0, concat_axis=0...  36.7 us
    all_to_all x1, starting transfers between devices, per_device(): lax.all_to_all(pack_slots(key_row_gradient), 'ctx', split_axis=0, concat_...  21.6 us
    all_to_all x1, waiting for transfers between devices, per_device(): lax.all_to_all(pack_slots(value_row_gradient), 'ctx', split_axis=0, conca...  16.4 us
    all_to_all x1, starting transfers between devices, per_device(): lax.all_to_all(pack_slots(value_row_gradient), 'ctx', split_axis=0, conca...  15.5 us
  transfers between devices with their start and end apart: 20, of which 11 were waited for; matrix products, arithmetic and copies ran while one was open for 23% of the time, Pallas kernels for 0%

commit v1 on v0

--- a/solution.py
+++ b/solution.py
@@ -163,7 +163,12 @@
     linear_value = arrived[2][inverse]
     result = (
         lax.all_to_all(linear_query, "head", split_axis=0, concat_axis=1, tiled=True),
-        lax.all_to_all(linear_key, "head", split_axis=0, concat_axis=1, tiled=True),
+        jnp.concatenate(
+            lax.all_to_all(
+                jnp.stack(jnp.split(linear_key, lax.axis_size("head"), axis=0)), "head", 0, 0
+            ),
+            axis=1,
+        ),
         lax.all_to_all(linear_value, "head", split_axis=0, concat_axis=1, tiled=True),
     )
     return (result[0], result[1], result[2])

time: 361 us -> 345 us (0.956)
  waiting for transfers between devices: 139 us -> 101 us
  starting transfers between devices: 132 us -> 151 us
    ppermute x8, waiting for transfers between devices: 57.1 us -> 23.3 us  [shifted(): return lax.ppermute(block, axis, route)]
    ppermute x8, starting transfers between devices: 40.5 us -> 54.2 us  [shifted(): return lax.ppermute(block, axis, route)]
    all_to_all x1, starting transfers between devices: 15.5 us -> 20.2 us  [per_device(): lax.all_to_all(pack_slots(value_row_gradient), 'ctx', split_axis=0, conca...]
    all_to_all x1, waiting for transfers between devices: 16.4 us -> 12.3 us  [per_device(): lax.all_to_all(pack_slots(value_row_gradient), 'ctx', split_axis=0, conca...]
    unnamed x34 -> x31, local copies, waits for them, and re-layouts: 2.71 us -> 6.35 us
  transfers between devices with their start and end apart: 20 -> 20, of which waited for: 11 -> 9; matrix products, arithmetic and copies ran while one was open for 23% -> 25% of each run, Pallas kernels for 0% -> 0%
where the time goes in v1:
time: 345 us; the launch traced here: 344 us
  starting transfers between devices  151 us (44%)
  waiting for transfers between devices  101 us (29%)
  local copies, waits for them, and re-layouts  80.5 us (23%)
  matrix products  5.96 us (2%)
  other arithmetic  4.01 us (1%)
    scatter x1, local copies, waits for them, and re-layouts, per_device(): inverse = jnp.zeros((length,), jnp.int32).at[where_to.reshape(-1)].set(so...  60.3 us
    ppermute x8, starting transfers between devices, shifted(): return lax.ppermute(block, axis, route)  54.2 us
    all_to_all x1, waiting for transfers between devices, per_device(): lax.all_to_all(pack_slots(query_grad), 'ctx', split_axis=0, concat_axis=0...  36.7 us
    ppermute x6, starting transfers between devices, from_behind(): return lax.ppermute(shard, axis, pairs)  36.6 us
    ppermute x8, waiting for transfers between devices, shifted(): return lax.ppermute(block, axis, route)  23.3 us
    all_to_all x1, starting transfers between devices, per_device(): lax.all_to_all(pack_slots(key_row_gradient), 'ctx', split_axis=0, concat_...  20.3 us
    all_to_all x1, starting transfers between devices, per_device(): lax.all_to_all(pack_slots(value_row_gradient), 'ctx', split_axis=0, conca...  20.2 us
    all_to_all x1, waiting for transfers between devices, per_device(): lax.all_to_all(linear_query, 'head', split_axis=0, concat_axis=1, tiled=T...  14.3 us
  transfers between devices with their start and end apart: 20, of which 9 were waited for; matrix products, arithmetic and copies ran while one was open for 25% of the time, Pallas kernels for 0%

profile of v1, /device:TPU:32, one launch (start us, length us, event | category | flops | bytes accessed | tf_op | source)
XLA Modules:
  0.0 344.2 jit_solution(291650036474579016)
XLA Ops:
  0.6 1.9 collective-permute-start.1
  2.5 15.1 %collective-permute-start = (bf16[256,128]{1,0:T(8,128)(2,1)}, bf16[256,128]{1,0:T(8,128)(2,1)S(1)}, u32[]{:S(2)}, u32[]{:S(2)}) collective-permute-start(bf16[256,128]{1,0:T(8,128)(2,1)} %param.9), channel_id=1, source_target_pairs={{0,8},{8,16},{16,24},{24,32},{32,40},{40,48},{48,56},{56,64},{64,7... | collective-permute-start | bytes 196616 | tf_op jit(solution)/shard_map/ppermute | solution.py:13
  17.7 0.6 copy-done.9
  18.6 1.1 convert_multiply_fusion
  22.9 2.1 collective-permute-start.6
  25.2 1.9 collective-permute-start.10
  27.7 0.6 reduce-window.24
  28.9 0.6 reduce-window.32
  29.9 60.3 %scatter_custom_fusion.1 = s32[256]{0:T(256)S(1)} fusion(s32[16384]{0:T(1024)S(1)} %compare_select_fusion, s32[16384]{0:T(1024)S(1)} %add.156, s32[]{:T(128)} %constant.73.clone.1), kind=kCustom, calls=%fused_computation.201 | custom fusion | bytes 1028 | tf_op jit(solution)/shard_map/scatter | solution.py:159
  90.3 1.9 collective-permute-start.3
  92.2 13.8 %collective-permute-start.2 = (bf16[256,128]{1,0:T(8,128)(2,1)S(1)}, bf16[256,128]{1,0:T(8,128)(2,1)S(1)}, u32[]{:S(2)}, u32[]{:S(2)}) collective-permute-start(bf16[256,128]{1,0:T(8,128)(2,1)S(1)} %collective-permute-done), channel_id=1, source_target_pairs={{0,8},{8,16},{16,24},{24,32},{32,40},{40,48},{48,56},{56,64},{64,7... | collective-permute-start | bytes 196616 | tf_op jit(solution)/shard_map/ppermute | solution.py:13
  107.3 1.9 collective-permute-start.7
  109.3 1.9 collective-permute-start.4
  112.5 14.6 %collective-permute-start.11 = (f32[256,128]{1,0:T(8,128)S(1)}, f32[256,128]{1,0:T(8,128)S(1)}, u32[]{:S(2)}, u32[]{:S(2)}) collective-permute-start(f32[256,128]{1,0:T(8,128)S(1)} %fusion.46), channel_id=1, source_target_pairs={{504,0},{0,8},{8,16},{16,24},{24,32},{32,40},{40,48},{48,56},{56,6... | collective-permute-start | bytes 393224 | tf_op jit(solution)/shard_map/ppermute | solution.py:19
  127.1 1.9 collective-permute-start.5
  130.2 3.5 %collective-permute-start.8 = (f32[256,128]{1,0:T(8,128)S(1)}, f32[256,128]{1,0:T(8,128)S(1)}, u32[]{:S(2)}, u32[]{:S(2)}) collective-permute-start(f32[256,128]{1,0:T(8,128)S(1)} %add.159), channel_id=1, source_target_pairs={{504,0},{0,8},{8,16},{16,24},{24,32},{32,40},{40,48},{48,56},{56,6... | collective-permute-start | bytes 393224 | tf_op jit(solution)/shard_map/ppermute | solution.py:19
  134.0 15.5 %collective-permute-done.8 = f32[256,128]{1,0:T(8,128)S(1)} collective-permute-done((f32[256,128]{1,0:T(8,128)S(1)}, f32[256,128]{1,0:T(8,128)S(1)}, u32[]{:S(2)}, u32[]{:S(2)}) %collective-permute-start.8) | collective-permute-done | bytes 131104 | tf_op jit(solution)/shard_map/ppermute | solution.py:19
  149.5 10.5 %collective-permute-start.9 = (bf16[256,128]{1,0:T(8,128)(2,1)S(1)}, bf16[256,128]{1,0:T(8,128)(2,1)}, u32[]{:S(2)}, u32[]{:S(2)}) collective-permute-start(bf16[256,128]{1,0:T(8,128)(2,1)S(1)} %add_convert_fusion.1), channel_id=1, source_target_pairs={{24,0},{32,8},{40,16},{48,24},{56,32},{64,40},{72,48},{80,56},{88,... | collective-permute-start | bytes 196616 | tf_op jit(solution)/shard_map/ppermute | solution.py:19
  160.3 12.9 %collective-permute-start.12 = (f32[256,128]{1,0:T(8,128)S(1)}, f32[256,128]{1,0:T(8,128)S(1)}, u32[]{:S(2)}, u32[]{:S(2)}) collective-permute-start(f32[256,128]{1,0:T(8,128)S(1)} %add.162), channel_id=1, source_target_pairs={{504,0},{0,8},{8,16},{16,24},{24,32},{32,40},{40,48},{48,56},{56,6... | collective-permute-start | bytes 393224 | tf_op jit(solution)/shard_map/ppermute | solution.py:19
  173.3 2.1 scatter_custom_fusion.2
  175.3 20.3 %all-to-all-start.2 = ((bf16[64,8,128]{2,1,0:T(8,128)(2,1)}), bf16[64,8,128]{2,1,0:T(8,128)(2,1)S(1)}, u32[]{:S(2)}, u32[]{:S(2)}) async-start(bf16[64,8,128]{2,1,0:T(8,128)(2,1)} %bitcast.50), calls=%async_computation.2 | async-start | bytes 262144 | tf_op jit(solution)/shard_map/all_to_all | solution.py:144
  196.0 6.8 %collective-permute-start.13 = (bf16[256,128]{1,0:T(8,128)(2,1)S(1)}, bf16[256,128]{1,0:T(8,128)(2,1)S(1)}, u32[]{:S(2)}, u32[]{:S(2)}) collective-permute-start(bf16[256,128]{1,0:T(8,128)(2,1)S(1)} %add_convert_fusion), channel_id=1, source_target_pairs={{24,0},{32,8},{40,16},{48,24},{56,32},{64,40},{72,48},{80,56},{88,... | collective-permute-start | bytes 196616 | tf_op jit(solution)/shard_map/ppermute | solution.py:19
  203.1 7.8 %collective-permute-done.13 = bf16[256,128]{1,0:T(8,128)(2,1)S(1)} collective-permute-done((bf16[256,128]{1,0:T(8,128)(2,1)S(1)}, bf16[256,128]{1,0:T(8,128)(2,1)S(1)}, u32[]{:S(2)}, u32[]{:S(2)}) %collective-permute-start.13) | collective-permute-done | bytes 65568 | tf_op jit(solution)/shard_map/ppermute | solution.py:19
  210.9 1.8 scatter_custom_fusion.3
  213.1 20.2 %all-to-all-start.4 = ((bf16[64,8,128]{2,1,0:T(8,128)(2,1)}), bf16[64,8,128]{2,1,0:T(8,128)(2,1)S(1)}, u32[]{:S(2)}, u32[]{:S(2)}) async-start(bf16[64,8,128]{2,1,0:T(8,128)(2,1)} %bitcast.69), calls=%async_computation.4 | async-start | bytes 262144 | tf_op jit(solution)/shard_map/all_to_all | solution.py:147
  233.4 0.9 gather_fusion.1
  234.2 0.6 constant_dynamic-update-slice_fusion.7
  234.8 0.6 constant_dynamic-update-slice_fusion.6
  235.4 0.6 constant_dynamic-update-slice_fusion.5
  236.0 0.6 constant_dynamic-update-slice_fusion.4
  236.6 0.6 constant_dynamic-update-slice_fusion.3
  237.2 0.6 constant_dynamic-update-slice_fusion.2
  237.8 0.6 constant_dynamic-update-slice_fusion.1
  239.0 12.3 %all-to-all-done.4 = bf16[64,8,128]{2,1,0:T(8,128)(2,1)S(1)} async-done(((bf16[64,8,128]{2,1,0:T(8,128)(2,1)}), bf16[64,8,128]{2,1,0:T(8,128)(2,1)S(1)}, u32[]{:S(2)}, u32[]{:S(2)}) %all-to-all-start.4) | async-done | bytes 131104 | tf_op jit(solution)/shard_map/all_to_all | solution.py:147
  251.4 5.7 %all-to-all-start.3 = ((bf16[8,32,128]{2,1,0:T(8,128)(2,1)}), bf16[8,32,128]{2,1,0:T(8,128)(2,1)S(1)}, u32[]{:S(2)}, u32[]{:S(2)}) async-start(bf16[8,32,128]{2,1,0:T(8,128)(2,1)} %constant_dynamic-update-slice_fusion), calls=%async_computation.3 | async-start | bytes 131072 | tf_op jit(solution)/shard_map/all_to_all | solution.py:167
  257.5 2.3 scatter_custom_fusion
  259.8 6.5 %all-to-all-done.3 = bf16[8,32,128]{2,1,0:T(8,128)(2,1)S(1)} async-done(((bf16[8,32,128]{2,1,0:T(8,128)(2,1)}), bf16[8,32,128]{2,1,0:T(8,128)(2,1)S(1)}, u32[]{:S(2)}, u32[]{:S(2)}) %all-to-all-start.3) | async-done | bytes 65568 | tf_op jit(solution)/shard_map/all_to_all | solution.py:167
  266.3 5.8 %all-to-all-start = ((bf16[64,8,512]{2,1,0:T(8,128)(2,1)}), bf16[64,8,512]{2,1,0:T(8,128)(2,1)S(1)}, u32[]{:S(2)}, u32[]{:S(2)}) async-start(bf16[64,8,512]{2,1,0:T(8,128)(2,1)} %bitcast.40), calls=%async_computation | async-start | bytes 1048576 | tf_op jit(solution)/shard_map/all_to_all | solution.py:143
  272.2 1.5 gather_fusion.2
  273.6 36.7 %all-to-all-done = bf16[64,8,512]{2,1,0:T(8,128)(2,1)S(1)} async-done(((bf16[64,8,512]{2,1,0:T(8,128)(2,1)}), bf16[64,8,512]{2,1,0:T(8,128)(2,1)S(1)}, u32[]{:S(2)}, u32[]{:S(2)}) %all-to-all-start) | async-done | bytes 524320 | tf_op jit(solution)/shard_map/all_to_all | solution.py:143
  310.4 3.3 all-to-all-start.5
  313.7 1.9 gather_fusion
  315.5 7.4 %all-to-all-done.5 = bf16[8,32,128]{2,1,0:T(8,128)(2,1)S(1)} async-done(((bf16[8,32,128]{2,1,0:T(8,128)(2,1)}), bf16[8,32,128]{2,1,0:T(8,128)(2,1)S(1)}, u32[]{:S(2)}, u32[]{:S(2)}) %all-to-all-start.5) | async-done | bytes 65568 | tf_op jit(solution)/shard_map/all_to_all | solution.py:172
  322.9 5.0 %all-to-all-start.1 = ((bf16[8,32,512]{2,1,0:T(8,128)(2,1)}), bf16[8,32,512]{2,1,0:T(8,128)(2,1)S(1)}, u32[]{:S(2)}, u32[]{:S(2)}) async-start(bf16[8,32,512]{2,1,0:T(8,128)(2,1)} %bitcast.44), calls=%async_computation.1 | async-start | bytes 524288 | tf_op jit(solution)/shard_map/all_to_all | solution.py:165
  327.9 0.6 copy_bitcast_fusion.1
  328.5 0.6 copy_bitcast_fusion
  329.1 14.3 %all-to-all-done.1 = bf16[8,32,512]{2,1,0:T(8,128)(2,1)S(1)} async-done(((bf16[8,32,512]{2,1,0:T(8,128)(2,1)}), bf16[8,32,512]{2,1,0:T(8,128)(2,1)S(1)}, u32[]{:S(2)}, u32[]{:S(2)}) %all-to-all-start.1) | async-done | bytes 262176 | tf_op jit(solution)/shard_map/all_to_all | solution.py:165
  343.4 0.7 copy.124
  (92 shorter events, 11.4 us)
Async XLA Ops:
  0.6 20.1 %copy-start = (bf16[256,512]{1,0:T(8,128)(2,1)S(1)}, bf16[256,512]{1,0:T(8,128)(2,1)}, u32[]{:S(2)}) copy-start(bf16[256,512]{1,0:T(8,128)(2,1)} %param.8) | copy-start | bytes 786436
  0.6 89.6 %collective-permute-start.1 = (bf16[256,128]{1,0:T(8,128)(2,1)}, bf16[256,128]{1,0:T(8,128)(2,1)S(1)}, u32[]{:S(2)}, u32[]{:S(2)}) collective-permute-start(bf16[256,128]{1,0:T(8,128)(2,1)} %param.10), channel_id=1, source_target_pairs={{0,8},{8,16},{16,24},{24,32},{32,40},{40,48},{48,56},{56,64},{64,7... | collective-permute-start | bytes 196616 | tf_op jit(solution)/shard_map/ppermute | solution.py:13
  2.5 89.7 %collective-permute-start = (bf16[256,128]{1,0:T(8,128)(2,1)}, bf16[256,128]{1,0:T(8,128)(2,1)S(1)}, u32[]{:S(2)}, u32[]{:S(2)}) collective-permute-start(bf16[256,128]{1,0:T(8,128)(2,1)} %param.9), channel_id=1, source_target_pairs={{0,8},{8,16},{16,24},{24,32},{32,40},{40,48},{48,56},{56,64},{64,7... | collective-permute-start | bytes 196616 | tf_op jit(solution)/shard_map/ppermute | solution.py:13
  17.7 0.7 copy-start.9
  20.5 0.8 copy-start.3
  20.5 0.8 copy-start.10
  21.3 1.0 copy-start.1
  21.3 1.0 copy-start.8
  22.8 4.3 %copy-start.2 = (s32[16384]{0:T(1024)S(1)}, s32[16384]{0:T(1024)}, u32[]{:S(2)}) copy-start(s32[16384]{0:T(1024)} %param.15) | copy-start | bytes 196612
  22.9 84.2 %collective-permute-start.6 = (f32[256,128]{1,0:T(8,128)S(1)}, f32[256,128]{1,0:T(8,128)S(1)}, u32[]{:S(2)}, u32[]{:S(2)}) collective-permute-start(f32[256,128]{1,0:T(8,128)S(1)} %convolution_bitcast_fusion.11), channel_id=1, source_target_pairs={{504,0},{0,8},{8,16},{16,24},{24,32},{32,40},{40,48},{48,56},{56,6... | collective-permute-start | bytes 393224 | tf_op jit(solution)/shard_map/ppermute | solution.py:19
  25.2 87.0 %collective-permute-start.10 = (f32[256,128]{1,0:T(8,128)S(1)}, f32[256,128]{1,0:T(8,128)S(1)}, u32[]{:S(2)}, u32[]{:S(2)}) collective-permute-start(f32[256,128]{1,0:T(8,128)S(1)} %convolution_bitcast_fusion.7), channel_id=1, source_target_pairs={{504,0},{0,8},{8,16},{16,24},{24,32},{32,40},{40,48},{48,56},{56,6... | collective-permute-start | bytes 393224 | tf_op jit(solution)/shard_map/ppermute | solution.py:19
  90.3 21.3 %collective-permute-start.3 = (bf16[256,128]{1,0:T(8,128)(2,1)S(1)}, bf16[256,128]{1,0:T(8,128)(2,1)S(1)}, u32[]{:S(2)}, u32[]{:S(2)}) collective-permute-start(bf16[256,128]{1,0:T(8,128)(2,1)S(1)} %collective-permute-done.1), channel_id=1, source_target_pairs={{0,8},{8,16},{16,24},{24,32},{32,40},{40,48},{48,56},{56,64},{64,7... | collective-permute-start | bytes 196616 | tf_op jit(solution)/shard_map/ppermute | solution.py:13
  92.2 17.1 %collective-permute-start.2 = (bf16[256,128]{1,0:T(8,128)(2,1)S(1)}, bf16[256,128]{1,0:T(8,128)(2,1)S(1)}, u32[]{:S(2)}, u32[]{:S(2)}) collective-permute-start(bf16[256,128]{1,0:T(8,128)(2,1)S(1)} %collective-permute-done), channel_id=1, source_target_pairs={{0,8},{8,16},{16,24},{24,32},{32,40},{40,48},{48,56},{56,64},{64,7... | collective-permute-start | bytes 196616 | tf_op jit(solution)/shard_map/ppermute | solution.py:13
  107.3 22.9 %collective-permute-start.7 = (f32[256,128]{1,0:T(8,128)S(1)}, f32[256,128]{1,0:T(8,128)S(1)}, u32[]{:S(2)}, u32[]{:S(2)}) collective-permute-start(f32[256,128]{1,0:T(8,128)S(1)} %fusion.45), channel_id=1, source_target_pairs={{504,0},{0,8},{8,16},{16,24},{24,32},{32,40},{40,48},{48,56},{56,6... | collective-permute-start | bytes 393224 | tf_op jit(solution)/shard_map/ppermute | solution.py:19
  109.3 2.3 copy-start.4
  109.3 19.7 %collective-permute-start.4 = (bf16[256,128]{1,0:T(8,128)(2,1)S(1)}, bf16[256,128]{1,0:T(8,128)(2,1)S(1)}, u32[]{:S(2)}, u32[]{:S(2)}) collective-permute-start(bf16[256,128]{1,0:T(8,128)(2,1)S(1)} %collective-permute-done.2), channel_id=1, source_target_pairs={{0,8},{8,16},{16,24},{24,32},{32,40},{40,48},{48,56},{56,64},{64,7... | collective-permute-start | bytes 196616 | tf_op jit(solution)/shard_map/ppermute | solution.py:13
  112.5 47.8 %collective-permute-start.11 = (f32[256,128]{1,0:T(8,128)S(1)}, f32[256,128]{1,0:T(8,128)S(1)}, u32[]{:S(2)}, u32[]{:S(2)}) collective-permute-start(f32[256,128]{1,0:T(8,128)S(1)} %fusion.46), channel_id=1, source_target_pairs={{504,0},{0,8},{8,16},{16,24},{24,32},{32,40},{40,48},{48,56},{56,6... | collective-permute-start | bytes 393224 | tf_op jit(solution)/shard_map/ppermute | solution.py:19
  127.1 2.8 collective-permute-start.5
  129.0 0.6 copy-start.6
  130.2 19.2 %collective-permute-start.8 = (f32[256,128]{1,0:T(8,128)S(1)}, f32[256,128]{1,0:T(8,128)S(1)}, u32[]{:S(2)}, u32[]{:S(2)}) collective-permute-start(f32[256,128]{1,0:T(8,128)S(1)} %add.159), channel_id=1, source_target_pairs={{504,0},{0,8},{8,16},{16,24},{24,32},{32,40},{40,48},{48,56},{56,6... | collective-permute-start | bytes 393224 | tf_op jit(solution)/shard_map/ppermute | solution.py:19
  149.5 23.8 %collective-permute-start.9 = (bf16[256,128]{1,0:T(8,128)(2,1)S(1)}, bf16[256,128]{1,0:T(8,128)(2,1)}, u32[]{:S(2)}, u32[]{:S(2)}) collective-permute-start(bf16[256,128]{1,0:T(8,128)(2,1)S(1)} %add_convert_fusion.1), channel_id=1, source_target_pairs={{24,0},{32,8},{40,16},{48,24},{56,32},{64,40},{72,48},{80,56},{88,... | collective-permute-start | bytes 196616 | tf_op jit(solution)/shard_map/ppermute | solution.py:19
  160.3 35.6 %collective-permute-start.12 = (f32[256,128]{1,0:T(8,128)S(1)}, f32[256,128]{1,0:T(8,128)S(1)}, u32[]{:S(2)}, u32[]{:S(2)}) collective-permute-start(f32[256,128]{1,0:T(8,128)S(1)} %add.162), channel_id=1, source_target_pairs={{504,0},{0,8},{8,16},{16,24},{24,32},{32,40},{40,48},{48,56},{56,6... | collective-permute-start | bytes 393224 | tf_op jit(solution)/shard_map/ppermute | solution.py:19
  175.3 37.8 %all-to-all-start.2 = ((bf16[64,8,128]{2,1,0:T(8,128)(2,1)}), bf16[64,8,128]{2,1,0:T(8,128)(2,1)S(1)}, u32[]{:S(2)}, u32[]{:S(2)}) async-start(bf16[64,8,128]{2,1,0:T(8,128)(2,1)} %bitcast.50), calls=%async_computation.2 | async-start | bytes 262144 | tf_op jit(solution)/shard_map/all_to_all | solution.py:144
  195.9 6.9 %copy-start.5 = (bf16[256,128]{1,0:T(8,128)(2,1)S(1)}, bf16[256,128]{1,0:T(8,128)(2,1)}, u32[]{:S(2)}) copy-start(bf16[256,128]{1,0:T(8,128)(2,1)} %copy-done.4) | copy-start | bytes 196612
  196.0 14.9 %collective-permute-start.13 = (bf16[256,128]{1,0:T(8,128)(2,1)S(1)}, bf16[256,128]{1,0:T(8,128)(2,1)S(1)}, u32[]{:S(2)}, u32[]{:S(2)}) collective-permute-start(bf16[256,128]{1,0:T(8,128)(2,1)S(1)} %add_convert_fusion), channel_id=1, source_target_pairs={{24,0},{32,8},{40,16},{48,24},{56,32},{64,40},{72,48},{80,56},{88,... | collective-permute-start | bytes 196616 | tf_op jit(solution)/shard_map/ppermute | solution.py:19
  213.1 38.2 %all-to-all-start.4 = ((bf16[64,8,128]{2,1,0:T(8,128)(2,1)}), bf16[64,8,128]{2,1,0:T(8,128)(2,1)S(1)}, u32[]{:S(2)}, u32[]{:S(2)}) async-start(bf16[64,8,128]{2,1,0:T(8,128)(2,1)} %bitcast.69), calls=%async_computation.4 | async-start | bytes 262144 | tf_op jit(solution)/shard_map/all_to_all | solution.py:147
  239.0 18.0 %copy-start.7 = (bf16[256,128]{1,0:T(8,128)(2,1)S(1)}, bf16[256,128]{1,0:T(8,128)(2,1)}, u32[]{:S(2)}) copy-start(bf16[256,128]{1,0:T(8,128)(2,1)} %copy-done.6) | copy-start | bytes 196612
  251.4 15.0 %all-to-all-start.3 = ((bf16[8,32,128]{2,1,0:T(8,128)(2,1)}), bf16[8,32,128]{2,1,0:T(8,128)(2,1)S(1)}, u32[]{:S(2)}, u32[]{:S(2)}) async-start(bf16[8,32,128]{2,1,0:T(8,128)(2,1)} %constant_dynamic-update-slice_fusion), calls=%async_computation.3 | async-start | bytes 131072 | tf_op jit(solution)/shard_map/all_to_all | solution.py:167
  266.3 44.0 %all-to-all-start = ((bf16[64,8,512]{2,1,0:T(8,128)(2,1)}), bf16[64,8,512]{2,1,0:T(8,128)(2,1)S(1)}, u32[]{:S(2)}, u32[]{:S(2)}) async-start(bf16[64,8,512]{2,1,0:T(8,128)(2,1)} %bitcast.40), calls=%async_computation | async-start | bytes 1048576 | tf_op jit(solution)/shard_map/all_to_all | solution.py:143
  310.4 12.6 %all-to-all-start.5 = ((bf16[8,32,128]{2,1,0:T(8,128)(2,1)}), bf16[8,32,128]{2,1,0:T(8,128)(2,1)S(1)}, u32[]{:S(2)}, u32[]{:S(2)}) async-start(bf16[8,32,128]{2,1,0:T(8,128)(2,1)} %bitcast.71), calls=%async_computation.5 | async-start | bytes 131072 | tf_op jit(solution)/shard_map/all_to_all | solution.py:172
  322.9 20.5 %all-to-all-start.1 = ((bf16[8,32,512]{2,1,0:T(8,128)(2,1)}), bf16[8,32,512]{2,1,0:T(8,128)(2,1)S(1)}, u32[]{:S(2)}, u32[]{:S(2)}) async-start(bf16[8,32,512]{2,1,0:T(8,128)(2,1)} %bitcast.44), calls=%async_computation.1 | async-start | bytes 524288 | tf_op jit(solution)/shard_map/all_to_all | solution.py:165
